TPU v7x, 32 devices: a whole 2x2x4 slice. The times are simulated.
32 devices in a mesh: grp: 2 (over x), smp: 16 (over z, y, core).
Axes of the slice: x: 2, y: 2, z: 4, core: 2. Of those that a mesh axis runs over, the one named last changes fastest.
Arguments:
- state: bfloat16 [512, 16, 1024], P(('grp', 'smp')), parts along dimension 0, may hold values from -40 to 40
- unit_slot: int32 [512, 64], P(('grp', 'smp')), parts along dimension 0, may hold values from 0 to 511
- token_count: int32 [512], P(('grp', 'smp')), parts along dimension 0, may hold values from 48 to 64, as said below
- session: int32 [512], P(('grp', 'smp')), parts along dimension 0, may hold values from 0 to 15, as said below
- session_row: int32 [32], P('grp'), parts along dimension 0, may hold values from 0 to 15, as said below
- unit_count: int32 [16], replicated, may hold values from 128 to 512, as said below
- panels: bfloat16 [16, 512, 1024], P('smp'), may hold values from -40 to 40
- memory_key: bfloat16 [512, 1024], P(('grp', 'smp')), parts along dimension 0, may hold values from -240 to 240
- memory_value: bfloat16 [512, 1024], P(('grp', 'smp')), parts along dimension 0, may hold values from -24 to 24
- q1_weight: bfloat16 [1024, 1024], replicated, may hold values from -0.1875 to 0.1875
- o1_weight: bfloat16 [1024, 1024], replicated, may hold values from -0.1875 to 0.1875
- kv_weight: bfloat16 [1024, 2048], replicated, may hold values from -6 to 6
- q2_weight: bfloat16 [1024, 1024], replicated, may hold values from -0.1875 to 0.1875
- o2_weight: bfloat16 [1024, 1024], replicated, may hold values from -0.1875 to 0.1875
Outputs:
- latent_out: bfloat16 [512, 16, 1024], P(('grp', 'smp')), parts along dimension 0
There are 2 independent parts, one for each index of `grp`. A program takes and returns all parts, laid end to end along the dimension named above; an argument that names none is the same for every part. Nothing has to cross between parts.
Inputs may be any that keep to these rules, and one draw needn't show every extreme that they name: The panel row of session s is session_row[s]; it lies on the device of index session_row[s]. session_row is a permutation. The 16 samples of one device have sessions on 16 different devices; one device holds the session of one sample on every device. `token_count`: some sample on every device has 64 tokens. `unit_count`: some panel row has 512 units.
All inputs are finite; a program needn't handle non-finite values.
Results may differ from a plain program's by a relative error of at most 0.007.
The roundings to bfloat16 on the way count: a program that leaves them out, or rounds other values in their place, can miss the bound.
Values may be sent and summed in bfloat16 or wider, within the bound.
No kernel may reach another device: no remote copies, remote signals or barrier semaphores. Data moves between devices by JAX's collectives and lax.ppermute only.
A program may use at most 128 MiB of HBM per device.

v0:
```python
import jax
import jax.numpy as jnp
from jax import lax
from jax.sharding import PartitionSpec as P

HEAD_DIM = 64
masked_score = -1e30


def normed(values):
    wide = values.astype(jnp.float32)
    return (wide * lax.rsqrt(jnp.mean(wide * wide, axis=-1, keepdims=True) + 1e-05)).astype(
        jnp.bfloat16
    )


def attend(queries, key_rows, value_rows, live_tokens):
    samples, latents, head_count, head_size = queries.shape
    spike_scores = jnp.einsum(
        "blhd,bkhd->bhlk", queries, key_rows, preferred_element_type=jnp.float32
    ) * HEAD_DIM ** (-0.5)
    spike_scores = jnp.where(live_tokens[:, None, None, :], spike_scores, masked_score)
    spike_max = jnp.max(spike_scores, axis=-1, keepdims=True)
    spike_exp = jnp.exp(spike_scores - spike_max)
    denominator = jnp.transpose(jnp.sum(spike_exp, axis=-1, keepdims=True), (0, 2, 1, 3))
    spike_mix = (
        jnp.einsum(
            "bhlk,bkhd->blhd",
            spike_exp.astype(jnp.bfloat16),
            value_rows,
            preferred_element_type=jnp.float32,
        )
        / denominator
    )
    return spike_mix.reshape(samples, latents, head_count * head_size).astype(jnp.bfloat16)


def per_device(
    state,
    unit_slot,
    token_count,
    session,
    session_row,
    unit_count,
    panels,
    memory_key,
    memory_value,
    q1_weight,
    o1_weight,
    kv_weight,
    q2_weight,
    o2_weight,
):
    local_samples, latents, model_width = state.shape
    token_total = unit_slot.shape[1]
    owners = lax.axis_size("smp")
    sess_dev, unit_total = (panels.shape[0], panels.shape[1])
    head_count = model_width // HEAD_DIM
    session_ids = jnp.arange(session_row.shape[0], dtype=jnp.int32)
    panel_row = jnp.sum(
        jnp.where(session[:, None] == session_ids[None, :], session_row[None, :], 0), axis=1
    )
    unit_limit = jnp.sum(
        jnp.where(panel_row[:, None] == session_ids[None, :], unit_count[None, :], 0), axis=1
    )
    owner_rank = panel_row // sess_dev
    token_index = (panel_row % sess_dev * unit_total)[:, None] + unit_slot % unit_limit[:, None]
    slot_pick = owner_rank[None, :] == jnp.arange(owners, dtype=jnp.int32)[:, None]
    request = jnp.sum(jnp.where(slot_pick[:, :, None], token_index[None, :, :], 0), axis=1)
    live_tokens = jnp.arange(token_total, dtype=jnp.int32)[None, :] < token_count[:, None]
    panel_table = panels.reshape(sess_dev * unit_total, model_width)
    arrived = lax.all_to_all(
        panel_table[lax.all_to_all(request, "smp", split_axis=0, concat_axis=0, tiled=True)],
        "smp",
        split_axis=0,
        concat_axis=0,
        tiled=True,
    )
    row_total = local_samples * latents
    flat_state = state.reshape(row_total, model_width)
    queries = jnp.dot(normed(flat_state), q1_weight, preferred_element_type=jnp.float32).astype(
        jnp.bfloat16
    )
    queries = queries.reshape(row_total, head_count, HEAD_DIM)
    running_max = jnp.full((head_count, row_total), masked_score, jnp.float32)
    key_rows = lax.all_gather(memory_key, "smp", axis=0, tiled=True).reshape(
        -1, head_count, HEAD_DIM
    )
    value_rows = lax.all_gather(memory_value, "smp", axis=0, tiled=True).reshape(
        -1, head_count, HEAD_DIM
    )
    scores = jnp.einsum(
        "rhd,khd->hrk", queries, key_rows, preferred_element_type=jnp.float32
    ) * HEAD_DIM ** (-0.5)
    new_max = jnp.maximum(running_max, jnp.max(scores, axis=-1))
    exponent = jnp.exp(scores - new_max[:, :, None])
    denominator = jnp.sum(exponent, axis=-1)
    weighted = jnp.einsum(
        "hrk,khd->hrd",
        exponent.astype(jnp.bfloat16),
        value_rows,
        preferred_element_type=jnp.float32,
    )
    running_max, denominator, weighted = (new_max, denominator, weighted)
    read_mem = (
        jnp.transpose(weighted / denominator[:, :, None], (1, 0, 2))
        .reshape(row_total, model_width)
        .astype(jnp.bfloat16)
    )
    hidden = (
        flat_state.astype(jnp.float32)
        + jnp.dot(read_mem, o1_weight, preferred_element_type=jnp.float32)
    ).astype(jnp.bfloat16)
    queries2 = jnp.dot(normed(hidden), q2_weight, preferred_element_type=jnp.float32).astype(
        jnp.bfloat16
    )
    queries2 = queries2.reshape(local_samples, latents, model_width)
    embed = arrived[owner_rank]
    key_value = jnp.dot(
        normed(embed.reshape(local_samples * token_total, model_width)),
        kv_weight,
        preferred_element_type=jnp.float32,
    ).astype(jnp.bfloat16)
    key_value = key_value.reshape(local_samples, token_total, 2 * model_width)
    key_rows = key_value[:, :, :model_width].reshape(
        local_samples, token_total, head_count, HEAD_DIM
    )
    value_rows = key_value[:, :, model_width:].reshape(
        local_samples, token_total, head_count, HEAD_DIM
    )
    read_spike = attend(
        queries2.reshape(local_samples, latents, head_count, HEAD_DIM),
        key_rows,
        value_rows,
        live_tokens,
    )
    result = hidden.astype(jnp.float32) + jnp.dot(
        read_spike.reshape(row_total, model_width), o2_weight, preferred_element_type=jnp.float32
    )
    return result.astype(jnp.bfloat16).reshape(local_samples, latents, model_width)


def solution(mesh):
    in_specs = (
        P(("grp", "smp"), None, None),
        P(("grp", "smp"), None),
        P(("grp", "smp")),
        P(("grp", "smp")),
        P("grp"),
        P(),
        P("smp", None, None),
        P(("grp", "smp"), None),
        P(("grp", "smp"), None),
        P(),
        P(),
        P(),
        P(),
        P(),
    )
    out_specs = P(("grp", "smp"), None, None)
    return jax.shard_map(
        per_device, mesh=mesh, in_specs=in_specs, out_specs=out_specs, check_vma=False
    )
```

profile of v0, /device:TPU:0, one launch (start us, length us, event | category | flops | bytes accessed | tf_op | source)
XLA Modules:
  0.0 167.4 jit_solution(13503824719128611106)
XLA Ops:
  0.0 0.0 copy-start
  0.0 1.0 select_reduce_fusion.2
  1.0 0.8 select_reduce_fusion.1
  1.9 0.9 add_select_fusion
  2.8 0.7 select_reduce_fusion
  3.5 7.4 %all-to-all-start = ((s32[16,1,64]{2,1,0:T(1,128)}), s32[16,1,64]{2,1,0:T(1,128)S(1)}, u32[]{:S(2)}, u32[]{:S(2)}) async-start(s32[16,1,64]{2,1,0:T(1,128)} %bitcast.9), calls=%async_computation | async-start | bytes 16384 | tf_op jit(solution)/shard_map/all_to_all | solution.py:73
  10.9 1.2 multiply_reduce_fusion.2
  12.1 5.1 %all-to-all-done = s32[16,1,64]{2,1,0:T(1,128)S(1)} async-done(((s32[16,1,64]{2,1,0:T(1,128)}), s32[16,1,64]{2,1,0:T(1,128)S(1)}, u32[]{:S(2)}, u32[]{:S(2)}) %all-to-all-start) | async-done | bytes 4128 | tf_op jit(solution)/shard_map/all_to_all | solution.py:73
  17.2 0.1 reshape.192
  17.3 7.4 %gather_fusion = bf16[1024,1024]{1,0:T(8,128)(2,1)} fusion(bf16[512,1024]{1,0:T(8,128)(2,1)} %bitcast.57, s32[1024]{0:T(1024)S(1)} %broadcast_clamp_fusion), kind=kCustom, calls=%fused_computation | custom fusion | bytes 4198400 | tf_op jit(solution)/shard_map/gather | solution.py:73
  24.7 0.0 copy-start.1
  24.7 4.6 %all-to-all-start.1 = ((bf16[16,64,1024]{2,1,0:T(8,128)(2,1)}), bf16[16,64,1024]{2,1,0:T(8,128)(2,1)}, u32[]{:S(2)}, u32[]{:S(2)}) async-start(bf16[16,64,1024]{2,1,0:T(8,128)(2,1)} %bitcast.58), calls=%async_computation.1 | async-start | bytes 4194304 | tf_op jit(solution)/shard_map/all_to_all | solution.py:72
  29.3 0.1 rsqrt.31
  29.4 0.0 copy-done.1
  29.4 0.2 fusion.31
  29.5 0.0 copy-start.5
  29.6 3.1 %convolution_convert_fusion.2 = bf16[256,1024]{1,0:T(8,128)(2,1)} fusion(bf16[256,1024]{1,0:T(8,128)(2,1)S(1)} %fusion.31, bf16[1024,1024]{1,0:T(8,128)(2,1)} %param.23), kind=kOutput, calls=%fused_computation.31 | convolution fusion | flops 537133056 | bytes 3145728 | tf_op jit(solution)/shard_map/dot_general | solution.py:81
  32.7 0.0 copy-start.6
  32.7 1.2 copy.36
  33.9 0.0 copy-done.5
  33.9 52.9 %all_gather.6 = bf16[256,1024]{1,0:T(8,128)(2,1)} all-gather(bf16[16,1024]{1,0:T(8,128)(2,1)S(1)} %copy-done.5), channel_id=1, replica_groups=mesh['grp'=2,'smp'=16] {'smp'}, dimensions={0}, use_global_device_ids=true | all-gather | bytes 557056 | tf_op jit(solution)/shard_map/all_gather | solution.py:86
  86.8 2.0 %copy.37 = bf16[256,1024]{0,1:T(8,128)(2,1)} copy(bf16[256,1024]{1,0:T(8,128)(2,1)} %all_gather.6) | data formatting | bytes 1048576 | tf_op jit(solution)/shard_map/all_gather | solution.py:86
  88.9 0.0 copy-done.6
  88.9 25.8 %all_gather.7 = bf16[256,1024]{1,0:T(8,128)(2,1)} all-gather(bf16[16,1024]{1,0:T(8,128)(2,1)S(1)} %copy-done.6), channel_id=1, replica_groups=mesh['grp'=2,'smp'=16] {'smp'}, dimensions={0}, use_global_device_ids=true | all-gather | bytes 557056 | tf_op jit(solution)/shard_map/all_gather | solution.py:89
  114.7 2.0 %copy.38 = bf16[256,1024]{0,1:T(8,128)(2,1)} copy(bf16[256,1024]{1,0:T(8,128)(2,1)} %all_gather.7) | data formatting | bytes 1048576 | tf_op jit(solution)/shard_map/all_gather | solution.py:89
  116.8 1.8 %multiply_reduce_fusion.1 = (f32[16,256]{1,0:T(8,128)S(1)}, f32[16,256,256]{1,2,0:T(8,128)S(1)}) fusion(bf16[256,16,64]{0,2,1:T(8,128)(2,1)S(1)} %bitcast.61, bf16[256,16,64]{0,2,1:T(8,128)(2,1)} %bitcast.62), kind=kOutput, calls=%fused_computation.10 | convolution fusion | flops 136310784 | bytes 5259264 | tf_op jit(solution)/shard_map/rhd,khd->hrk/dot_general | solution.py:92
  118.6 0.0 copy-start.3
  118.6 0.7 fusion.5
  119.3 0.3 copy-done.3
  119.6 0.9 fusion.25
  120.5 0.0 copy-start.9
  120.5 0.0 copy-done
  120.5 0.8 fusion.28
  121.4 0.0 copy-start.4
  121.4 0.8 copy-done.4
  122.2 0.0 copy-done.9
  122.2 0.0 copy-start.7
  122.2 1.6 convolution_convert_fusion.1
  123.8 1.8 %reshape_reshape.3 = bf16[16,16,16,64]{3,2,1,0:T(8,128)(2,1)S(1)} reshape(bf16[256,1024]{1,0:T(8,128)(2,1)} %convolution_convert_fusion.1) | data formatting | bytes 1048576 | tf_op jit(solution)/shard_map/reshape;reshape | solution.py:132
  125.5 0.0 copy-done.7
  125.6 0.1 iota_compare_fusion
  125.6 0.0 all-to-all-done.1
  125.6 3.6 %gather_fusion.1 = bf16[16,64,1024]{2,1,0:T(8,128)(2,1)} fusion(bf16[16,64,1024]{2,1,0:T(8,128)(2,1)} %all-to-all-done.1, s32[1024]{0:T(1024)S(1)} %pad_clamp_fusion), kind=kCustom, calls=%fused_computation.1 | custom fusion | bytes 4194368 | tf_op jit(solution)/shard_map/gather | solution.py:118
  129.2 2.1 %multiply_reduce_fusion = f32[16,64]{1,0:T(8,128)S(1)} fusion(bf16[16,64,1024]{2,1,0:T(8,128)(2,1)} %gather_fusion.1), kind=kLoop, calls=%fused_computation.8 | loop fusion | flops 3144704 | bytes 2101248 | tf_op jit(solution)/shard_map/reduce_sum | solution.py:12
  131.3 0.1 rsqrt.33
  131.4 0.0 copy-start.8
  131.4 2.1 %fusion = bf16[1024,1024]{1,0:T(8,128)(2,1)S(1)} fusion(f32[1024]{0:T(1024)S(1)} %rsqrt.33, bf16[16,64,1024]{2,1,0:T(8,128)(2,1)} %gather_fusion.1), kind=kLoop, calls=%fused_computation.3 | loop fusion | flops 3145728 | bytes 4198400 | tf_op jit(solution)/shard_map/convert_element_type | solution.py:12
  133.5 0.7 copy-done.8
  134.2 4.7 %convolution_convert_fusion = bf16[1024,2048]{1,0:T(8,128)(2,1)S(1)} fusion(bf16[1024,1024]{1,0:T(8,128)(2,1)S(1)} %fusion, bf16[1024,2048]{1,0:T(8,128)(2,1)S(1)} %copy-done.8), kind=kOutput, calls=%fused_computation.11 | convolution fusion | flops 4297064448 | bytes 10485760 | tf_op jit(solution)/shard_map/dot_general | solution.py:119
  138.9 2.6 %fusion.43 = (bf16[16,64,1024]{2,1,0:T(8,128)(2,1)}, bf16[16,64,1024]{2,1,0:T(8,128)(2,1)}) fusion(bf16[16,64,2048]{2,1,0:T(8,128)(2,1)S(1)} %bitcast.60), kind=kLoop, calls=%fused_computation.68 | loop fusion | bytes 8388608 | tf_op jit(solution)/shard_map/slice | solution.py:125
  141.5 6.4 %reshape.186 = bf16[16,64,16,64]{3,2,1,0:T(8,128)(2,1)} reshape(bf16[16,64,1024]{2,1,0:T(8,128)(2,1)} %get-tuple-element.5) | data formatting | bytes 4194304 | tf_op jit(solution)/shard_map/reshape | solution.py:125
  147.9 6.4 %reshape.185 = bf16[16,64,16,64]{3,2,1,0:T(8,128)(2,1)} reshape(bf16[16,64,1024]{2,1,0:T(8,128)(2,1)} %get-tuple-element.6) | data formatting | bytes 4194304 | tf_op jit(solution)/shard_map/reshape | solution.py:128
  154.3 0.0 copy-start.2
  154.3 4.7 %fusion.12 = (f32[16,16,16]{2,1,0:T(8,128)S(1)}, f32[16,16,16,64]{3,2,1,0:T(8,128)S(1)}) fusion(pred[16,64]{1,0:T(8,128)(4,1)S(1)} %iota_compare_fusion, bf16[16,64,16,64]{3,2,1,0:T(8,128)(2,1)} %reshape.186, bf16[16,16,16,64]{3,2,1,0:T(8,128)(2,1)S(1)} %reshape_reshape.3), kind=kOutput, calls=%fused_computation.21 | convolution fusion | flops 34336768 | bytes 3687424 | tf_op jit(solution)/shard_map/blhd,bkhd->bhlk/dot_general | solution.py:19
  159.0 1.3 fusion.15
  160.3 0.0 copy-done.2
  160.3 2.0 %fusion.9 = bf16[16,16,16,64]{3,1,2,0:T(8,128)(2,1)S(1)} fusion(bf16[16,64,16,64]{3,2,1,0:T(8,128)(2,1)S(1)} %copy-done.2, f32[16,16,16,64]{3,2,1,0:T(8,128)S(1)} %get-tuple-element.12, f32[16,16,16]{1,2,0:T(8,128)S(1)} %bitcast.65, f32[16,16,16]{2,1,0:T(8,128)S(1)} %get-tuple-element.11, pred[16,64]{1,0:T(8,128)(4,1)S(1)} %iota_compare_fusion), kind=kOutput, calls=%fused_computation.16 | convolution fusion | flops 35127296 | bytes 3703808 | tf_op jit(solution)/shard_map/bhlk,bkhd->blhd/dot_general | solution.py:27
  162.3 0.3 copy.44
  162.6 1.5 convert_element_type.85
  164.1 3.3 %fusion.20 = bf16[256,1024]{1,0:T(8,128)(2,1)} fusion(bf16[256,1024]{1,0:T(8,128)(2,1)} %convert_element_type.85, bf16[1024,1024]{1,0:T(8,128)(2,1)} %param.27, bf16[256,1024]{1,0:T(8,128)(2,1)} %copy-done.4), kind=kOutput, calls=%fused_computation.29 | convolution fusion | flops 537657344 | bytes 3670016 | tf_op jit(solution)/shard_map/dot_general | solution.py:137
  (11 shorter events, 0.1 us)
Async XLA Ops:
  0.0 120.5 %copy-start = (bf16[1024,1024]{1,0:T(8,128)(2,1)S(1)}, bf16[1024,1024]{1,0:T(8,128)(2,1)}, u32[]{:S(2)}) copy-start(bf16[1024,1024]{1,0:T(8,128)(2,1)} %param.24) | copy-start | bytes 6291460
  3.5 13.7 %all-to-all-start = ((s32[16,1,64]{2,1,0:T(1,128)}), s32[16,1,64]{2,1,0:T(1,128)S(1)}, u32[]{:S(2)}, u32[]{:S(2)}) async-start(s32[16,1,64]{2,1,0:T(1,128)} %bitcast.9), calls=%async_computation | async-start | bytes 16384 | tf_op jit(solution)/shard_map/all_to_all | solution.py:73
  24.7 4.7 %copy-start.1 = (bf16[16,16,1024]{2,1,0:T(8,128)(2,1)S(1)}, bf16[16,16,1024]{2,1,0:T(8,128)(2,1)}, u32[]{:S(2)}) copy-start(bf16[16,16,1024]{2,1,0:T(8,128)(2,1)} %param.14) | copy-start | bytes 1572868
  24.7 100.9 %all-to-all-start.1 = ((bf16[16,64,1024]{2,1,0:T(8,128)(2,1)}), bf16[16,64,1024]{2,1,0:T(8,128)(2,1)}, u32[]{:S(2)}, u32[]{:S(2)}) async-start(bf16[16,64,1024]{2,1,0:T(8,128)(2,1)} %bitcast.58), calls=%async_computation.1 | async-start | bytes 4194304 | tf_op jit(solution)/shard_map/all_to_all | solution.py:72
  29.5 4.4 %copy-start.5 = (bf16[16,1024]{1,0:T(8,128)(2,1)S(1)}, bf16[16,1024]{1,0:T(8,128)(2,1)}, u32[]{:S(2)}) copy-start(bf16[16,1024]{1,0:T(8,128)(2,1)} %param.21) | copy-start | bytes 98308
  32.7 56.2 %copy-start.6 = (bf16[16,1024]{1,0:T(8,128)(2,1)S(1)}, bf16[16,1024]{1,0:T(8,128)(2,1)}, u32[]{:S(2)}) copy-start(bf16[16,1024]{1,0:T(8,128)(2,1)} %param.22) | copy-start | bytes 98308
  118.6 1.0 copy-start.3
  120.5 1.7 %copy-start.9 = (bf16[1024,1024]{1,0:T(8,128)(2,1)S(1)}, bf16[1024,1024]{1,0:T(8,128)(2,1)}, u32[]{:S(2)}) copy-start(bf16[1024,1024]{1,0:T(8,128)(2,1)} %param.26) | copy-start | bytes 6291460
  121.4 0.8 copy-start.4
  122.2 3.4 %copy-start.7 = (s32[16]{0:T(128)S(1)}, s32[16]{0:T(128)}, u32[]{:S(2)}) copy-start(s32[16]{0:T(128)} %param.16) | copy-start | bytes 196
  131.4 2.8 %copy-start.8 = (bf16[1024,2048]{1,0:T(8,128)(2,1)S(1)}, bf16[1024,2048]{1,0:T(8,128)(2,1)}, u32[]{:S(2)}) copy-start(bf16[1024,2048]{1,0:T(8,128)(2,1)} %param.25) | copy-start | bytes 12582916
  154.3 6.1 %copy-start.2 = (bf16[16,64,16,64]{3,2,1,0:T(8,128)(2,1)S(1)}, bf16[16,64,16,64]{3,2,1,0:T(8,128)(2,1)}, u32[]{:S(2)}) copy-start(bf16[16,64,16,64]{3,2,1,0:T(8,128)(2,1)} %reshape.185) | copy-start | bytes 6291460
where the time goes:
time: 168 us; the launch traced here: 167 us
  blocking collectives  78.8 us (47%)
  local copies, waits for them, and re-layouts  37.3 us (22%)
  matrix products  22.9 us (14%)
  starting transfers between devices  11.9 us (7%)
  other arithmetic  11.2 us (7%)
  waiting for transfers between devices  5.11 us (3%)
    all_gather x1, blocking collectives, per_device(): lax.all_gather(memory_key, 'smp', axis=0, tiled=True)  52.9 us
    all_gather x1, blocking collectives, per_device(): lax.all_gather(memory_value, 'smp', axis=0, tiled=True)  25.8 us
    gather x1, local copies, waits for them, and re-layouts, per_device(): panel_table[lax.all_to_all(request, 'smp', split_axis=0, concat_axis=0, t...  7.42 us
    all_to_all x1, starting transfers between devices, per_device(): lax.all_to_all(request, 'smp', split_axis=0, concat_axis=0, tiled=True)  7.39 us
    reshape x1, local copies, waits for them, and re-layouts, per_device(): key_value[:, :, :model_width]  6.37 us
    reshape x1, local copies, waits for them, and re-layouts, per_device(): key_value[:, :, model_width:]  6.37 us
    all_to_all x1, waiting for transfers between devices, per_device(): lax.all_to_all(request, 'smp', split_axis=0, concat_axis=0, tiled=True)  5.11 us
    dot_general x1, matrix products, per_device(): jnp.dot(normed(embed.reshape(local_samples * token_total, model_width)),...  4.71 us
  transfers between devices with their start and end apart: 2, of which 1 were waited for; matrix products, arithmetic and copies ran while one was open for 10% of the time, Pallas kernels for 0%

commit v1 on v0

--- a/solution.py
+++ b/solution.py
@@ -69,13 +69,20 @@
     request = jnp.sum(jnp.where(slot_pick[:, :, None], token_index[None, :, :], 0), axis=1)
     live_tokens = jnp.arange(token_total, dtype=jnp.int32)[None, :] < token_count[:, None]
     panel_table = panels.reshape(sess_dev * unit_total, model_width)
-    arrived = lax.all_to_all(
-        panel_table[lax.all_to_all(request, "smp", split_axis=0, concat_axis=0, tiled=True)],
-        "smp",
-        split_axis=0,
-        concat_axis=0,
-        tiled=True,
-    )
+    value = panel_table[lax.all_to_all(request, "smp", split_axis=0, concat_axis=0, tiled=True)]
+    ways, here = (lax.axis_size("smp"), lax.axis_index("smp"))
+    width = value.shape[0] // ways
+    lengths = list(value.shape)
+    lengths[0] = width
+    height = lengths[0]
+    lengths[0] = height * ways
+    full = jnp.zeros(lengths, value.dtype)
+    for mask in range(ways):
+        part = lax.dynamic_slice_in_dim(value, (here ^ mask) * width, width, axis=0)
+        if mask:
+            part = lax.ppermute(part, "smp", [(d, d ^ mask) for d in range(ways)])
+        full = lax.dynamic_update_slice_in_dim(full, part, (here ^ mask) * height, axis=0)
+    arrived = full
     row_total = local_samples * latents
     flat_state = state.reshape(row_total, model_width)
     queries = jnp.dot(normed(flat_state), q1_weight, preferred_element_type=jnp.float32).astype(

time: 168 us -> 184 us (1.095)
  the two profiles are of different devices: /device:TPU:0 before, /device:TPU:9 now
where the time goes in v1:
time: 184 us; the launch traced here: 183 us
  local copies, waits for them, and re-layouts  47.6 us (26%)
  starting transfers between devices  41.4 us (22%)
  blocking collectives  40.5 us (22%)
  matrix products  23 us (12%)
  waiting for transfers between devices  15.5 us (8%)
  other arithmetic  14.6 us (8%)
    ppermute x15, starting transfers between devices, per_device(): part = lax.ppermute(part, 'smp', [(d, d ^ mask) for d in range(ways)])  34.8 us
    all_gather x1, blocking collectives, per_device(): lax.all_gather(memory_key, 'smp', axis=0, tiled=True)  21.6 us
    all_gather x1, blocking collectives, per_device(): lax.all_gather(memory_value, 'smp', axis=0, tiled=True)  18.9 us
    ppermute x15, waiting for transfers between devices, per_device(): part = lax.ppermute(part, 'smp', [(d, d ^ mask) for d in range(ways)])  15.4 us
    dynamic_update_slice x15, local copies, waits for them, and re-layouts, per_device(): lax.dynamic_update_slice_in_dim(full, part, (here ^ mask) * height, axis=0)  11.7 us
    all_to_all x1, starting transfers between devices, per_device(): lax.all_to_all(request, 'smp', split_axis=0, concat_axis=0, tiled=True)  6.61 us
    reshape x1, local copies, waits for them, and re-layouts, per_device(): key_value[:, :, model_width:]  6.41 us
    reshape x1, local copies, waits for them, and re-layouts, per_device(): key_value[:, :, :model_width]  6.35 us
  transfers between devices with their start and end apart: 16, of which 5 were waited for; matrix products, arithmetic and copies ran while one was open for 15% of the time, Pallas kernels for 0%

profile of v1, /device:TPU:9, one launch (start us, length us, event | category | flops | bytes accessed | tf_op | source)
XLA Modules:
  0.0 182.8 jit_solution(10450941866318423545)
XLA Ops:
  0.0 1.0 select_reduce_fusion.2
  1.0 0.8 select_reduce_fusion.1
  1.9 0.9 add_select_fusion
  2.8 0.7 select_reduce_fusion
  3.5 6.6 %all-to-all-start = ((s32[16,1,64]{2,1,0:T(1,128)}), s32[16,1,64]{2,1,0:T(1,128)S(1)}, u32[]{:S(2)}, u32[]{:S(2)}) async-start(s32[16,1,64]{2,1,0:T(1,128)} %bitcast.9), calls=%async_computation | async-start | bytes 16384 | tf_op jit(solution)/shard_map/all_to_all | solution.py:72
  10.1 1.2 multiply_reduce_fusion.2
  11.4 1.2 fusion.31
  12.6 2.3 %convolution_convert_fusion.2 = bf16[256,1024]{1,0:T(8,128)(2,1)S(1)} fusion(bf16[256,1024]{1,0:T(8,128)(2,1)S(1)} %fusion.31, bf16[1024,1024]{1,0:T(8,128)(2,1)} %param.23), kind=kOutput, calls=%fused_computation.31 | convolution fusion | flops 537133056 | bytes 3145728 | tf_op jit(solution)/shard_map/dot_general | solution.py:88
  15.2 21.6 %all_gather.6 = bf16[256,1024]{1,0:T(8,128)(2,1)} all-gather(bf16[16,1024]{1,0:T(8,128)(2,1)S(1)} %copy-done.8), channel_id=1, replica_groups=mesh['grp'=2,'smp'=16] {'smp'}, dimensions={0}, use_global_device_ids=true | all-gather | bytes 557056 | tf_op jit(solution)/shard_map/all_gather | solution.py:93
  36.8 1.2 copy.37
  38.0 2.7 %multiply_reduce_fusion.1 = (f32[16,256]{1,0:T(8,128)S(1)}, f32[16,256,256]{1,2,0:T(8,128)}) fusion(bf16[256,16,64]{0,2,1:T(8,128)(2,1)S(1)} %bitcast.61, bf16[256,16,64]{0,2,1:T(8,128)(2,1)S(1)} %bitcast.62), kind=kOutput, calls=%fused_computation.10 | convolution fusion | flops 136310784 | bytes 5259264 | tf_op jit(solution)/shard_map/rhd,khd->hrk/dot_general | solution.py:99
  40.7 18.9 %all_gather.7 = bf16[256,1024]{1,0:T(8,128)(2,1)S(1)} all-gather(bf16[16,1024]{1,0:T(8,128)(2,1)S(1)} %copy-done.9), channel_id=1, replica_groups=mesh['grp'=2,'smp'=16] {'smp'}, dimensions={0}, use_global_device_ids=true | all-gather | bytes 557056 | tf_op jit(solution)/shard_map/all_gather | solution.py:96
  59.8 3.0 %fusion.5 = f32[16,256]{1,0:T(8,128)S(1)} fusion(f32[16,256,256]{1,2,0:T(8,128)} %get-tuple-element.24, f32[16,256]{1,0:T(8,128)S(1)} %broadcast_maximum_fusion), kind=kLoop, calls=%fused_computation.12 | loop fusion | flops 3141632 | bytes 4227072 | tf_op jit(solution)/shard_map/reduce_sum | solution.py:104
  63.3 0.9 fusion.25
  64.3 0.8 fusion.28
  65.2 0.8 copy-done.7
  66.0 1.6 convolution_convert_fusion.1
  67.8 5.5 %gather_fusion = bf16[1024,1024]{1,0:T(8,128)(2,1)} fusion(bf16[512,1024]{1,0:T(8,128)(2,1)S(1)} %bitcast.57, s32[1024]{0:T(1024)S(1)} %broadcast_clamp_fusion), kind=kCustom, calls=%fused_computation | custom fusion | bytes 4198400 | tf_op jit(solution)/shard_map/gather | solution.py:72
  73.5 1.3 copy-done.3
  74.8 1.2 constant_dynamic-slice_fusion
  76.0 1.3 copy-done.4
  77.5 1.4 collective-permute-start.1
  79.0 1.8 reshape_reshape.3
  81.3 3.0 %collective-permute-start.3 = (bf16[1,64,1024]{2,1,0:T(8,128)(2,1)}, bf16[1,64,1024]{2,1,0:T(8,128)(2,1)S(1)}, u32[]{:S(2)}, u32[]{:S(2)}) collective-permute-start(bf16[1,64,1024]{2,1,0:T(8,128)(2,1)} %get-tuple-element.18), channel_id=1, source_target_pairs={{0,4},{1,5},{2,6},{3,7},{4,0},{5,1},{6,2},{7,3},{8,12},{9,13},{10,... | collective-permute-start | bytes 393224 | tf_op jit(solution)/shard_map/ppermute | solution.py:83
  84.4 2.5 %collective-permute-start.5 = (bf16[1,64,1024]{2,1,0:T(8,128)(2,1)}, bf16[1,64,1024]{2,1,0:T(8,128)(2,1)S(1)}, u32[]{:S(2)}, u32[]{:S(2)}) collective-permute-start(bf16[1,64,1024]{2,1,0:T(8,128)(2,1)} %get-tuple-element.16), channel_id=1, source_target_pairs={{0,6},{1,7},{2,4},{3,5},{4,2},{5,3},{6,0},{7,1},{8,14},{9,15},{10,... | collective-permute-start | bytes 393224 | tf_op jit(solution)/shard_map/ppermute | solution.py:83
  87.0 1.6 constant_dynamic-update-slice_fusion.13
  88.9 1.6 constant_dynamic-update-slice_fusion.12
  90.6 0.7 constant_dynamic-update-slice_fusion.11
  91.3 2.6 %collective-permute-start.8 = (bf16[1,64,1024]{2,1,0:T(8,128)(2,1)}, bf16[1,64,1024]{2,1,0:T(8,128)(2,1)S(1)}, u32[]{:S(2)}, u32[]{:S(2)}) collective-permute-start(bf16[1,64,1024]{2,1,0:T(8,128)(2,1)} %get-tuple-element.13), channel_id=1, source_target_pairs={{0,9},{1,8},{2,11},{3,10},{4,13},{5,12},{6,15},{7,14},{8,1},{9,0},... | collective-permute-start | bytes 393224 | tf_op jit(solution)/shard_map/ppermute | solution.py:83
  93.9 0.7 constant_dynamic-update-slice_fusion.10
  94.6 1.2 collective-permute-start.9
  95.8 0.7 constant_dynamic-update-slice_fusion.9
  96.4 4.3 %collective-permute-start.10 = (bf16[1,64,1024]{2,1,0:T(8,128)(2,1)}, bf16[1,64,1024]{2,1,0:T(8,128)(2,1)S(1)}, u32[]{:S(2)}, u32[]{:S(2)}) collective-permute-start(bf16[1,64,1024]{2,1,0:T(8,128)(2,1)} %get-tuple-element.11), channel_id=1, source_target_pairs={{0,11},{1,10},{2,9},{3,8},{4,15},{5,14},{6,13},{7,12},{8,3},{9,2},... | collective-permute-start | bytes 393224 | tf_op jit(solution)/shard_map/ppermute | solution.py:83
  100.8 0.7 constant_dynamic-update-slice_fusion.8
  101.4 0.7 constant_dynamic-update-slice_fusion.7
  102.1 9.4 %collective-permute-start.12 = (bf16[1,64,1024]{2,1,0:T(8,128)(2,1)S(1)}, bf16[1,64,1024]{2,1,0:T(8,128)(2,1)S(1)}, u32[]{:S(2)}, u32[]{:S(2)}) collective-permute-start(bf16[1,64,1024]{2,1,0:T(8,128)(2,1)S(1)} %get-tuple-element.9), channel_id=1, source_target_pairs={{0,13},{1,12},{2,15},{3,14},{4,9},{5,8},{6,11},{7,10},{8,5},{9,4},... | collective-permute-start | bytes 393224 | tf_op jit(solution)/shard_map/ppermute | solution.py:83
  111.5 0.7 constant_dynamic-update-slice_fusion.6
  112.2 2.2 %collective-permute-start.13 = (bf16[1,64,1024]{2,1,0:T(8,128)(2,1)S(1)}, bf16[1,64,1024]{2,1,0:T(8,128)(2,1)S(1)}, u32[]{:S(2)}, u32[]{:S(2)}) collective-permute-start(bf16[1,64,1024]{2,1,0:T(8,128)(2,1)S(1)} %get-tuple-element.8), channel_id=1, source_target_pairs={{0,14},{1,15},{2,12},{3,13},{4,10},{5,11},{6,8},{7,9},{8,6},{9,7},... | collective-permute-start | bytes 393224 | tf_op jit(solution)/shard_map/ppermute | solution.py:83
  114.4 0.7 constant_dynamic-update-slice_fusion.5
  115.1 2.0 %collective-permute-done.9 = bf16[1,64,1024]{2,1,0:T(8,128)(2,1)S(1)} collective-permute-done((bf16[1,64,1024]{2,1,0:T(8,128)(2,1)}, bf16[1,64,1024]{2,1,0:T(8,128)(2,1)S(1)}, u32[]{:S(2)}, u32[]{:S(2)}) %collective-permute-start.9) | collective-permute-done | bytes 131104 | tf_op jit(solution)/shard_map/ppermute | solution.py:83
  117.1 6.5 %collective-permute-start.14 = (bf16[1,64,1024]{2,1,0:T(8,128)(2,1)S(1)}, bf16[1,64,1024]{2,1,0:T(8,128)(2,1)S(1)}, u32[]{:S(2)}, u32[]{:S(2)}) collective-permute-start(bf16[1,64,1024]{2,1,0:T(8,128)(2,1)S(1)} %get-tuple-element.7), channel_id=1, source_target_pairs={{0,15},{1,14},{2,13},{3,12},{4,11},{5,10},{6,9},{7,8},{8,7},{9,6},... | collective-permute-start | bytes 393224 | tf_op jit(solution)/shard_map/ppermute | solution.py:83
  123.6 0.7 constant_dynamic-update-slice_fusion.4
  124.3 0.7 constant_dynamic-update-slice_fusion.3
  125.0 5.4 %collective-permute-done.11 = bf16[1,64,1024]{2,1,0:T(8,128)(2,1)S(1)} collective-permute-done((bf16[1,64,1024]{2,1,0:T(8,128)(2,1)}, bf16[1,64,1024]{2,1,0:T(8,128)(2,1)S(1)}, u32[]{:S(2)}, u32[]{:S(2)}) %collective-permute-start.11) | collective-permute-done | bytes 131104 | tf_op jit(solution)/shard_map/ppermute | solution.py:83
  130.4 0.7 constant_dynamic-update-slice_fusion.2
  131.1 3.0 %collective-permute-done.12 = bf16[1,64,1024]{2,1,0:T(8,128)(2,1)S(1)} collective-permute-done((bf16[1,64,1024]{2,1,0:T(8,128)(2,1)S(1)}, bf16[1,64,1024]{2,1,0:T(8,128)(2,1)S(1)}, u32[]{:S(2)}, u32[]{:S(2)}) %collective-permute-start.12) | collective-permute-done | bytes 131104 | tf_op jit(solution)/shard_map/ppermute | solution.py:83
  134.1 0.7 constant_dynamic-update-slice_fusion.1
  134.7 2.8 %collective-permute-done.13 = bf16[1,64,1024]{2,1,0:T(8,128)(2,1)S(1)} collective-permute-done((bf16[1,64,1024]{2,1,0:T(8,128)(2,1)S(1)}, bf16[1,64,1024]{2,1,0:T(8,128)(2,1)S(1)}, u32[]{:S(2)}, u32[]{:S(2)}) %collective-permute-start.13) | collective-permute-done | bytes 131104 | tf_op jit(solution)/shard_map/ppermute | solution.py:83
  137.5 0.6 constant_dynamic-update-slice_fusion
  138.2 2.2 %collective-permute-done.14 = bf16[1,64,1024]{2,1,0:T(8,128)(2,1)S(1)} collective-permute-done((bf16[1,64,1024]{2,1,0:T(8,128)(2,1)S(1)}, bf16[1,64,1024]{2,1,0:T(8,128)(2,1)S(1)}, u32[]{:S(2)}, u32[]{:S(2)}) %collective-permute-start.14) | collective-permute-done | bytes 131104 | tf_op jit(solution)/shard_map/ppermute | solution.py:83
  140.3 0.7 constant_dynamic-update-slice_fusion.14
  141.0 3.6 %gather_fusion.1 = bf16[16,64,1024]{2,1,0:T(8,128)(2,1)} fusion(bf16[16,64,1024]{2,1,0:T(8,128)(2,1)} %constant_dynamic-update-slice_fusion.14, s32[1024]{0:T(1024)S(1)} %pad_clamp_fusion), kind=kCustom, calls=%fused_computation.1 | custom fusion | bytes 4194368 | tf_op jit(solution)/shard_map/gather | solution.py:125
  144.6 2.1 %multiply_reduce_fusion = f32[16,64]{1,0:T(8,128)S(1)} fusion(bf16[16,64,1024]{2,1,0:T(8,128)(2,1)} %gather_fusion.1), kind=kLoop, calls=%fused_computation.8 | loop fusion | flops 3144704 | bytes 2101248 | tf_op jit(solution)/shard_map/reduce_sum | solution.py:12
  146.7 2.1 %fusion = bf16[1024,1024]{1,0:T(8,128)(2,1)S(1)} fusion(f32[1024]{0:T(1024)S(1)} %rsqrt.33, bf16[16,64,1024]{2,1,0:T(8,128)(2,1)} %gather_fusion.1), kind=kLoop, calls=%fused_computation.3 | loop fusion | flops 3145728 | bytes 4198400 | tf_op jit(solution)/shard_map/convert_element_type | solution.py:12
  148.9 0.7 copy-done.11
  149.5 4.7 %convolution_convert_fusion = bf16[1024,2048]{1,0:T(8,128)(2,1)S(1)} fusion(bf16[1024,1024]{1,0:T(8,128)(2,1)S(1)} %fusion, bf16[1024,2048]{1,0:T(8,128)(2,1)S(1)} %copy-done.11), kind=kOutput, calls=%fused_computation.11 | convolution fusion | flops 4297064448 | bytes 10485760 | tf_op jit(solution)/shard_map/dot_general | solution.py:126
  154.3 2.6 %fusion.43 = (bf16[16,64,1024]{2,1,0:T(8,128)(2,1)}, bf16[16,64,1024]{2,1,0:T(8,128)(2,1)}) fusion(bf16[16,64,2048]{2,1,0:T(8,128)(2,1)S(1)} %bitcast.60), kind=kLoop, calls=%fused_computation.99 | loop fusion | bytes 8388608 | tf_op jit(solution)/shard_map/slice | solution.py:132
  156.8 6.4 %reshape.186 = bf16[16,64,16,64]{3,2,1,0:T(8,128)(2,1)} reshape(bf16[16,64,1024]{2,1,0:T(8,128)(2,1)} %get-tuple-element.5) | data formatting | bytes 4194304 | tf_op jit(solution)/shard_map/reshape | solution.py:132
  163.2 6.4 %reshape.185 = bf16[16,64,16,64]{3,2,1,0:T(8,128)(2,1)} reshape(bf16[16,64,1024]{2,1,0:T(8,128)(2,1)} %get-tuple-element.6) | data formatting | bytes 4194304 | tf_op jit(solution)/shard_map/reshape | solution.py:135
  169.6 4.7 %fusion.12 = (f32[16,16,16]{2,1,0:T(8,128)S(1)}, f32[16,16,16,64]{3,2,1,0:T(8,128)S(1)}) fusion(pred[16,64]{1,0:T(8,128)(4,1)S(1)} %iota_compare_fusion, bf16[16,64,16,64]{3,2,1,0:T(8,128)(2,1)} %reshape.186, bf16[16,16,16,64]{3,2,1,0:T(8,128)(2,1)S(1)} %reshape_reshape.3), kind=kOutput, calls=%fused_computation.21 | convolution fusion | flops 34336768 | bytes 3687424 | tf_op jit(solution)/shard_map/blhd,bkhd->bhlk/dot_general | solution.py:19
  174.3 1.3 fusion.15
  175.6 2.0 %fusion.9 = bf16[16,16,16,64]{3,1,2,0:T(8,128)(2,1)S(1)} fusion(bf16[16,64,16,64]{3,2,1,0:T(8,128)(2,1)S(1)} %copy-done.6, f32[16,16,16,64]{3,2,1,0:T(8,128)S(1)} %get-tuple-element.28, f32[16,16,16]{1,2,0:T(8,128)S(1)} %bitcast.65, f32[16,16,16]{2,1,0:T(8,128)S(1)} %get-tuple-element.27, pred[16,64]{1,0:T(8,128)(4,1)S(1)} %iota_compare_fusion), kind=kOutput, calls=%fused_computation.16 | convolution fusion | flops 35127296 | bytes 3703808 | tf_op jit(solution)/shard_map/bhlk,bkhd->blhd/dot_general | solution.py:27
  177.9 1.5 convert_element_type.85
  179.4 3.3 %fusion.20 = bf16[256,1024]{1,0:T(8,128)(2,1)} fusion(bf16[256,1024]{1,0:T(8,128)(2,1)} %convert_element_type.85, bf16[1024,1024]{1,0:T(8,128)(2,1)} %param.27, bf16[256,1024]{1,0:T(8,128)(2,1)} %copy-done.7), kind=kOutput, calls=%fused_computation.29 | convolution fusion | flops 537657344 | bytes 3670016 | tf_op jit(solution)/shard_map/dot_general | solution.py:144
  (58 shorter events, 3.3 us)
Async XLA Ops:
  0.0 64.2 %copy-start = (bf16[1024,1024]{1,0:T(8,128)(2,1)S(1)}, bf16[1024,1024]{1,0:T(8,128)(2,1)}, u32[]{:S(2)}) copy-start(bf16[1024,1024]{1,0:T(8,128)(2,1)} %param.24) | copy-start | bytes 6291460
  3.5 64.2 %all-to-all-start = ((s32[16,1,64]{2,1,0:T(1,128)}), s32[16,1,64]{2,1,0:T(1,128)S(1)}, u32[]{:S(2)}, u32[]{:S(2)}) async-start(s32[16,1,64]{2,1,0:T(1,128)} %bitcast.9), calls=%async_computation | async-start | bytes 16384 | tf_op jit(solution)/shard_map/all_to_all | solution.py:72
  12.6 2.5 %copy-start.8 = (bf16[16,1024]{1,0:T(8,128)(2,1)S(1)}, bf16[16,1024]{1,0:T(8,128)(2,1)}, u32[]{:S(2)}) copy-start(bf16[16,1024]{1,0:T(8,128)(2,1)} %param.21) | copy-start | bytes 98308
  38.0 2.7 %copy-start.9 = (bf16[16,1024]{1,0:T(8,128)(2,1)S(1)}, bf16[16,1024]{1,0:T(8,128)(2,1)}, u32[]{:S(2)}) copy-start(bf16[16,1024]{1,0:T(8,128)(2,1)} %param.22) | copy-start | bytes 98308
  59.8 3.5 %copy-start.2 = (f32[16,256,256]{1,2,0:T(8,128)S(1)}, f32[16,256,256]{1,2,0:T(8,128)}, u32[]{:S(2)}) copy-start(f32[16,256,256]{1,2,0:T(8,128)} %get-tuple-element.24) | copy-start | bytes 12582916
  63.3 1.0 copy-start.5
  64.2 1.8 copy-start.12
  65.2 0.8 copy-start.7
  65.2 2.4 %copy-start.10 = (s32[16]{0:T(128)S(1)}, s32[16]{0:T(128)}, u32[]{:S(2)}) copy-start(s32[16]{0:T(128)} %param.16) | copy-start | bytes 196
  65.2 2.6 %copy-start.1 = (bf16[1,512,1024]{2,1,0:T(8,128)(2,1)S(1)}, bf16[1,512,1024]{2,1,0:T(8,128)(2,1)}, u32[]{:S(2)}) copy-start(bf16[1,512,1024]{2,1,0:T(8,128)(2,1)} %param.20) | copy-start | bytes 3145732
  73.2 1.6 copy-start.3
  76.0 1.3 copy-start.4
  77.3 7.1 %collective-permute-start = (bf16[1,64,1024]{2,1,0:T(8,128)(2,1)}, bf16[1,64,1024]{2,1,0:T(8,128)(2,1)}, u32[]{:S(2)}, u32[]{:S(2)}) collective-permute-start(bf16[1,64,1024]{2,1,0:T(8,128)(2,1)} %get-tuple-element.21), channel_id=1, source_target_pairs={{0,1},{1,0},{2,3},{3,2},{4,5},{5,4},{6,7},{7,6},{8,9},{9,8},{10,11... | collective-permute-start | bytes 393224 | tf_op jit(solution)/shard_map/ppermute | solution.py:83
  77.5 11.0 %collective-permute-start.1 = (bf16[1,64,1024]{2,1,0:T(8,128)(2,1)}, bf16[1,64,1024]{2,1,0:T(8,128)(2,1)}, u32[]{:S(2)}, u32[]{:S(2)}) collective-permute-start(bf16[1,64,1024]{2,1,0:T(8,128)(2,1)} %get-tuple-element.20), channel_id=1, source_target_pairs={{0,2},{1,3},{2,0},{3,1},{4,6},{5,7},{6,4},{7,5},{8,10},{9,11},{10,... | collective-permute-start | bytes 393224 | tf_op jit(solution)/shard_map/ppermute | solution.py:83
  80.7 9.7 %collective-permute-start.2 = (bf16[1,64,1024]{2,1,0:T(8,128)(2,1)}, bf16[1,64,1024]{2,1,0:T(8,128)(2,1)S(1)}, u32[]{:S(2)}, u32[]{:S(2)}) collective-permute-start(bf16[1,64,1024]{2,1,0:T(8,128)(2,1)} %get-tuple-element.19), channel_id=1, source_target_pairs={{0,3},{1,2},{2,1},{3,0},{4,7},{5,6},{6,5},{7,4},{8,11},{9,10},{10,... | collective-permute-start | bytes 393224 | tf_op jit(solution)/shard_map/ppermute | solution.py:83
  81.3 10.0 %collective-permute-start.3 = (bf16[1,64,1024]{2,1,0:T(8,128)(2,1)}, bf16[1,64,1024]{2,1,0:T(8,128)(2,1)S(1)}, u32[]{:S(2)}, u32[]{:S(2)}) collective-permute-start(bf16[1,64,1024]{2,1,0:T(8,128)(2,1)} %get-tuple-element.18), channel_id=1, source_target_pairs={{0,4},{1,5},{2,6},{3,7},{4,0},{5,1},{6,2},{7,3},{8,12},{9,13},{10,... | collective-permute-start | bytes 393224 | tf_op jit(solution)/shard_map/ppermute | solution.py:83
  84.3 10.3 %collective-permute-start.4 = (bf16[1,64,1024]{2,1,0:T(8,128)(2,1)}, bf16[1,64,1024]{2,1,0:T(8,128)(2,1)S(1)}, u32[]{:S(2)}, u32[]{:S(2)}) collective-permute-start(bf16[1,64,1024]{2,1,0:T(8,128)(2,1)} %get-tuple-element.17), channel_id=1, source_target_pairs={{0,5},{1,4},{2,7},{3,6},{4,1},{5,0},{6,3},{7,2},{8,13},{9,12},{10,... | collective-permute-start | bytes 393224 | tf_op jit(solution)/shard_map/ppermute | solution.py:83
  84.4 12.0 %collective-permute-start.5 = (bf16[1,64,1024]{2,1,0:T(8,128)(2,1)}, bf16[1,64,1024]{2,1,0:T(8,128)(2,1)S(1)}, u32[]{:S(2)}, u32[]{:S(2)}) collective-permute-start(bf16[1,64,1024]{2,1,0:T(8,128)(2,1)} %get-tuple-element.16), channel_id=1, source_target_pairs={{0,6},{1,7},{2,4},{3,5},{4,2},{5,3},{6,0},{7,1},{8,14},{9,15},{10,... | collective-permute-start | bytes 393224 | tf_op jit(solution)/shard_map/ppermute | solution.py:83
  88.5 12.9 %collective-permute-start.6 = (bf16[1,64,1024]{2,1,0:T(8,128)(2,1)}, bf16[1,64,1024]{2,1,0:T(8,128)(2,1)S(1)}, u32[]{:S(2)}, u32[]{:S(2)}) collective-permute-start(bf16[1,64,1024]{2,1,0:T(8,128)(2,1)} %get-tuple-element.15), channel_id=1, source_target_pairs={{0,7},{1,6},{2,5},{3,4},{4,3},{5,2},{6,1},{7,0},{8,15},{9,14},{10,... | collective-permute-start | bytes 393224 | tf_op jit(solution)/shard_map/ppermute | solution.py:83
  90.4 11.7 %collective-permute-start.7 = (bf16[1,64,1024]{2,1,0:T(8,128)(2,1)}, bf16[1,64,1024]{2,1,0:T(8,128)(2,1)S(1)}, u32[]{:S(2)}, u32[]{:S(2)}) collective-permute-start(bf16[1,64,1024]{2,1,0:T(8,128)(2,1)} %get-tuple-element.14), channel_id=1, source_target_pairs={{0,8},{1,9},{2,10},{3,11},{4,12},{5,13},{6,14},{7,15},{8,0},{9,1},... | collective-permute-start | bytes 393224 | tf_op jit(solution)/shard_map/ppermute | solution.py:83
  91.3 20.9 %collective-permute-start.8 = (bf16[1,64,1024]{2,1,0:T(8,128)(2,1)}, bf16[1,64,1024]{2,1,0:T(8,128)(2,1)S(1)}, u32[]{:S(2)}, u32[]{:S(2)}) collective-permute-start(bf16[1,64,1024]{2,1,0:T(8,128)(2,1)} %get-tuple-element.13), channel_id=1, source_target_pairs={{0,9},{1,8},{2,11},{3,10},{4,13},{5,12},{6,15},{7,14},{8,1},{9,0},... | collective-permute-start | bytes 393224 | tf_op jit(solution)/shard_map/ppermute | solution.py:83
  94.6 22.5 %collective-permute-start.9 = (bf16[1,64,1024]{2,1,0:T(8,128)(2,1)}, bf16[1,64,1024]{2,1,0:T(8,128)(2,1)S(1)}, u32[]{:S(2)}, u32[]{:S(2)}) collective-permute-start(bf16[1,64,1024]{2,1,0:T(8,128)(2,1)} %get-tuple-element.12), channel_id=1, source_target_pairs={{0,10},{1,11},{2,8},{3,9},{4,14},{5,15},{6,12},{7,13},{8,2},{9,3},... | collective-permute-start | bytes 393224 | tf_op jit(solution)/shard_map/ppermute | solution.py:83
  96.4 27.9 %collective-permute-start.10 = (bf16[1,64,1024]{2,1,0:T(8,128)(2,1)}, bf16[1,64,1024]{2,1,0:T(8,128)(2,1)S(1)}, u32[]{:S(2)}, u32[]{:S(2)}) collective-permute-start(bf16[1,64,1024]{2,1,0:T(8,128)(2,1)} %get-tuple-element.11), channel_id=1, source_target_pairs={{0,11},{1,10},{2,9},{3,8},{4,15},{5,14},{6,13},{7,12},{8,3},{9,2},... | collective-permute-start | bytes 393224 | tf_op jit(solution)/shard_map/ppermute | solution.py:83
  101.4 29.0 %collective-permute-start.11 = (bf16[1,64,1024]{2,1,0:T(8,128)(2,1)}, bf16[1,64,1024]{2,1,0:T(8,128)(2,1)S(1)}, u32[]{:S(2)}, u32[]{:S(2)}) collective-permute-start(bf16[1,64,1024]{2,1,0:T(8,128)(2,1)} %get-tuple-element.10), channel_id=1, source_target_pairs={{0,12},{1,13},{2,14},{3,15},{4,8},{5,9},{6,10},{7,11},{8,4},{9,5},... | collective-permute-start | bytes 393224 | tf_op jit(solution)/shard_map/ppermute | solution.py:83
  102.1 32.0 %collective-permute-start.12 = (bf16[1,64,1024]{2,1,0:T(8,128)(2,1)S(1)}, bf16[1,64,1024]{2,1,0:T(8,128)(2,1)S(1)}, u32[]{:S(2)}, u32[]{:S(2)}) collective-permute-start(bf16[1,64,1024]{2,1,0:T(8,128)(2,1)S(1)} %get-tuple-element.9), channel_id=1, source_target_pairs={{0,13},{1,12},{2,15},{3,14},{4,9},{5,8},{6,11},{7,10},{8,5},{9,4},... | collective-permute-start | bytes 393224 | tf_op jit(solution)/shard_map/ppermute | solution.py:83
  112.2 25.3 %collective-permute-start.13 = (bf16[1,64,1024]{2,1,0:T(8,128)(2,1)S(1)}, bf16[1,64,1024]{2,1,0:T(8,128)(2,1)S(1)}, u32[]{:S(2)}, u32[]{:S(2)}) collective-permute-start(bf16[1,64,1024]{2,1,0:T(8,128)(2,1)S(1)} %get-tuple-element.8), channel_id=1, source_target_pairs={{0,14},{1,15},{2,12},{3,13},{4,10},{5,11},{6,8},{7,9},{8,6},{9,7},... | collective-permute-start | bytes 393224 | tf_op jit(solution)/shard_map/ppermute | solution.py:83
  117.1 23.2 %collective-permute-start.14 = (bf16[1,64,1024]{2,1,0:T(8,128)(2,1)S(1)}, bf16[1,64,1024]{2,1,0:T(8,128)(2,1)S(1)}, u32[]{:S(2)}, u32[]{:S(2)}) collective-permute-start(bf16[1,64,1024]{2,1,0:T(8,128)(2,1)S(1)} %get-tuple-element.7), channel_id=1, source_target_pairs={{0,15},{1,14},{2,13},{3,12},{4,11},{5,10},{6,9},{7,8},{8,7},{9,6},... | collective-permute-start | bytes 393224 | tf_op jit(solution)/shard_map/ppermute | solution.py:83
  146.7 2.8 %copy-start.11 = (bf16[1024,2048]{1,0:T(8,128)(2,1)S(1)}, bf16[1024,2048]{1,0:T(8,128)(2,1)}, u32[]{:S(2)}) copy-start(bf16[1024,2048]{1,0:T(8,128)(2,1)} %param.25) | copy-start | bytes 12582916
  169.6 6.1 %copy-start.6 = (bf16[16,64,16,64]{3,2,1,0:T(8,128)(2,1)S(1)}, bf16[16,64,16,64]{3,2,1,0:T(8,128)(2,1)}, u32[]{:S(2)}) copy-start(bf16[16,64,16,64]{3,2,1,0:T(8,128)(2,1)} %reshape.185) | copy-start | bytes 6291460
